TPU v7x, 512 devices: a whole 4x8x8 slice. The times are simulated.
512 devices in a mesh: sub: 128 (over z, y, core), harm: 4 (over x).
Axes of the slice: x: 4, y: 8, z: 8, core: 2. Of those that a mesh axis runs over, the one named last changes fastest.
Arguments:
- lengths: int32 [384], P('sub'), may hold values from 128 to 1024, as said below
- owners: int32 [384, 1], P('sub'), may hold values from 0 to 127, as said below
- front_inverse: bfloat16 [384, 1024, 1024], P('sub', 'harm'), may hold values from -0.1875 to 0.1875
- coupling: bfloat16 [384, 1024, 768], P('sub', 'harm'), may hold values from -0.1875 to 0.1875
- stiffness: bfloat16 [384, 768, 768], P('sub', 'harm'), may hold values from -0.21875 to 0.21875
- displacement: bfloat16 [128, 32, 768], P('sub', 'harm'), may hold values from -6 to 6
- forcing: float32 [128, 32, 768], P('sub', 'harm'), may hold values from -6 to 6
- lumped_mass: float32 [128, 768], P('sub'), may hold values from 0.2 to 2
- damping: float32 [128, 768], P('sub'), may hold values from 0.1 to 1.5
Outputs:
- interior: bfloat16 [384, 32, 1024], P('sub', None, 'harm')
- residual: float32 [128, 32, 768], P('sub', 'harm')
- modes: bfloat16 [384, 1024, 768], P('sub', 'harm')
Inputs may be any that keep to these rules, and one draw needn't show every extreme that they name: `lengths`: live interior front rows of each substructure, which are its first rows; some substructure has all 1024. `owners`: substructure k lies on sub index k // 3; on every sub index d, the first 2 of its 3 substructures are attached to block (d + 64) mod 128, the third to a block of uneven popularity; every interface block has at least one substructure.
All inputs are finite; a program needn't handle non-finite values.
Results may differ from a plain program's by a relative error of at most 0.008.
Values may be sent and summed in bfloat16 or wider, within the bound.
No kernel may reach another device: no remote copies, remote signals or barrier semaphores. Data moves between devices by JAX's collectives and lax.ppermute only.
A program may use at most 64 MiB of HBM per device.

v0:
```python
import jax
import jax.numpy as jnp
from jax import lax
from jax.sharding import Mesh
from jax.sharding import PartitionSpec as P

SUB = ("sub_0", "sub_1", "sub_2")
PLANE = ("sub_0", "sub_1")
PAIR = ("sub_2", "harm")


def copy_for_each(x, axis):
    length = lax.axis_size(axis)
    return lax.all_to_all(jnp.broadcast_to(x[None], (length, *x.shape)), axis, 0, 0, tiled=True)


def joined_along(tiles, dim):
    tiles = jnp.moveaxis(tiles, 0, dim)
    shape = tiles.shape
    return tiles.reshape(*shape[:dim], shape[dim] * shape[dim + 1], *shape[dim + 2 :])


def whole_of(x, axes, dim):
    far, near = axes
    tiles = copy_for_each(copy_for_each(x, far), near)
    return joined_along(tiles.swapaxes(0, 1).reshape(-1, *x.shape), dim)


def collect(x, axis, dim):
    tiles = copy_for_each(x, axis)
    return joined_along(tiles, dim)


def in_blocks(x, dim, length):
    shape = x.shape
    tiles = x.reshape(*shape[:dim], length, shape[dim] // length, *shape[dim + 1 :])
    return jnp.moveaxis(tiles, dim, 0)


def sent_and_summed(x, axis, dim):
    tiles = in_blocks(x, dim, lax.axis_size(axis))
    arrived = lax.all_to_all(tiles, axis, split_axis=0, concat_axis=0, tiled=True)
    return arrived.astype(jnp.float32).sum(axis=0)


def body(
    lengths, owners, front_inverse, coupling, stiffness, displacement, forcing, lumped_mass, damping
):
    nharm = lax.axis_size("harm")
    harm_idx = lax.axis_index("harm")
    front_q = coupling.shape[1]
    width = coupling.shape[2]
    width_q = stiffness.shape[1]
    nown = lax.axis_size(SUB)
    own_rows = harm_idx * front_q + jnp.arange(front_q, dtype=jnp.int32)
    live_rows = own_rows[None, :] < lengths[:, None]
    masked = jnp.where(live_rows[:, :, None], coupling, jnp.zeros_like(coupling))
    piece = lax.all_gather(coupling, "harm", axis=1, tiled=True)
    live_cols = jnp.arange(nharm * front_q, dtype=jnp.int32)[None, :] < lengths[:, None]
    front_live = jnp.where(live_cols[:, None, :], front_inverse, jnp.zeros_like(front_inverse))
    modes = jnp.einsum(
        "sfg,sgn->sfn", front_live, piece, preferred_element_type=jnp.float32
    ).astype(jnp.bfloat16)
    nplane = lax.axis_size(PLANE)
    rows_q = displacement.shape[1]
    core = lax.axis_index("sub_2")
    near = (lax.axis_index(SUB) + nown // 2) % nown
    third = owners[2, 0]
    other = lax.ppermute(owners[2:3, 0], "sub_2", [(0, 1), (1, 0)])[0]
    plane = copy_for_each(displacement[0], PLANE)
    lent = lax.ppermute(
        lax.dynamic_index_in_dim(plane, other // 2, 0, keepdims=False), "sub_2", [(0, 1), (1, 0)]
    )
    here = lax.dynamic_index_in_dim(plane, third // 2, 0, keepdims=False)
    picked = jnp.stack(
        [
            lax.dynamic_index_in_dim(plane, near // 2, 0, keepdims=False),
            jnp.where(third % 2 == core, here, lent),
        ]
    )
    own_pair = collect(picked, "harm", 1)
    own_disp = jnp.stack([own_pair[0], own_pair[0], own_pair[1]])
    inner = -jnp.einsum("sfn,shn->shf", modes, own_disp, preferred_element_type=jnp.float32)
    interior = jnp.where(live_rows[:, None, :], inner, jnp.float32(0.0)).astype(jnp.bfloat16)
    disp_cols = lax.dynamic_slice_in_dim(own_disp, harm_idx * width_q, width_q, 2)
    contrib = jnp.einsum("shf,sfn->shn", interior, masked, preferred_element_type=jnp.float32)
    contrib = contrib + jnp.einsum(
        "shj,sjn->shn", disp_cols, stiffness, preferred_element_type=jnp.float32
    )
    near_c = (contrib[0] + contrib[1]).reshape(nharm, rows_q, width)
    third_c = contrib[2].reshape(nharm, rows_q, width)
    zero_rows = jnp.zeros_like(near_c)
    send = jnp.stack(
        [
            jnp.stack(
                [
                    jnp.where(peer_core == core, near_c, zero_rows),
                    jnp.where(third % 2 == peer_core, third_c, zero_rows),
                ],
                axis=1,
            )
            for peer_core in range(2)
        ]
    )
    came = lax.all_to_all(
        send.reshape(2 * nharm, 2, rows_q, width).astype(jnp.bfloat16), PAIR, 0, 0, tiled=True
    ).astype(jnp.float32)
    came = came.reshape(2, nharm, 2, rows_q, width).sum(axis=1)
    mine = jnp.where(core == 0, came[0], came[1])
    theirs = jnp.where(core == 0, came[1], came[0])
    near_part = mine[0]
    third_part = mine[1]
    other_part = theirs[1]
    slots = jnp.arange(nplane, dtype=jnp.int32)[:, None, None]
    dense = (
        jnp.where(slots == near // 2, near_part, jnp.float32(0.0))
        + jnp.where((slots == third // 2) & (third % 2 == core), third_part, jnp.float32(0.0))
        + jnp.where((slots == other // 2) & (other % 2 == core), other_part, jnp.float32(0.0))
    )
    arrived = lax.all_to_all(
        dense.astype(jnp.bfloat16), PLANE, split_axis=0, concat_axis=0, tiled=True
    ).astype(jnp.float32)
    gathered = jnp.sum(arrived, axis=0, keepdims=True)
    rows_q = displacement.shape[1]
    pairs_all = rows_q * nharm // 2
    rows = harm_idx * rows_q + jnp.arange(rows_q, dtype=jnp.int32)
    pair = (rows // 2).astype(jnp.float32)
    parity = (rows % 2).astype(jnp.float32)
    freq = 1.5 * (pair + 1.0) / pairs_all
    sign = 1.0 - 2.0 * parity
    disp = displacement.astype(jnp.float32)
    partner = disp.reshape(1, rows_q // 2, 2, width)[:, :, ::-1, :].reshape(1, rows_q, width)
    residual = (
        gathered
        - (freq * freq)[None, :, None] * lumped_mass[:, None, :] * disp
        + (sign * freq)[None, :, None] * damping[:, None, :] * partner
        - forcing
    )
    return (interior, residual, modes)


def solution(mesh):
    split = Mesh(
        mesh.devices.reshape(8, 8, 2, mesh.shape["harm"]), ("sub_0", "sub_1", "sub_2", "harm")
    )
    placed = (
        P(SUB),
        P(SUB, None),
        P(SUB, "harm", None),
        P(SUB, "harm", None),
        P(SUB, "harm", None),
        P(SUB, "harm", None),
        P(SUB, "harm", None),
        P(SUB, None),
        P(SUB, None),
    )
    return jax.shard_map(
        body,
        mesh=split,
        in_specs=placed,
        out_specs=(P(SUB, None, "harm"), P(SUB, "harm", None), P(SUB, "harm", None)),
        check_vma=False,
    )
```

profile of v0, /device:TPU:8, one launch (start us, length us, event | category | flops | bytes accessed | tf_op | source)
XLA Modules:
  0.0 136.1 jit_solution(10824814379573062923)
XLA Ops:
  7.2 0.7 all-gather.2.cloned.1.call-update
  7.9 1.6 %broadcast_in_dim.101 = bf16[64,8,768]{2,1,0:T(8,128)(2,1)} broadcast(bf16[8,768]{1,0:T(8,128)(2,1)} %bitcast.58), dimensions={1,2} | broadcast | bytes 798720 | tf_op jit(solution)/shard_map/broadcast_in_dim | solution.py:14
  9.6 16.6 %all-to-all-start = ((bf16[64,8,768]{2,1,0:T(8,128)(2,1)}), bf16[64,8,768]{2,1,0:T(8,128)(2,1)S(1)}, u32[]{:S(2)}, u32[]{:S(2)}) async-start(bf16[64,8,768]{2,1,0:T(8,128)(2,1)} %broadcast_in_dim.101), calls=%async_computation | async-start | bytes 1572864 | tf_op jit(solution)/shard_map/all_to_all | solution.py:14
  26.2 0.6 slice.46
  26.8 1.9 %collective-permute-start = (s32[1]{0:T(128)}, s32[1]{0:T(128)}, u32[]{:S(2)}, u32[]{:S(2)}) collective-permute-start(s32[1]{0:T(128)} %bitcast.3), channel_id=1, source_target_pairs={{0,4},{4,0},{1,5},{5,1},{2,6},{6,2},{3,7},{7,3},{8,12},{12,8},{9,1... | collective-permute-start | bytes 20 | tf_op jit(solution)/shard_map/ppermute | solution.py:69
  28.8 1.1 collective-permute-done
  32.4 17.7 %all-to-all-done = bf16[64,8,768]{2,1,0:T(8,128)(2,1)S(1)} async-done(((bf16[64,8,768]{2,1,0:T(8,128)(2,1)}), bf16[64,8,768]{2,1,0:T(8,128)(2,1)S(1)}, u32[]{:S(2)}, u32[]{:S(2)}) %all-to-all-start) | async-done | bytes 786464 | tf_op jit(solution)/shard_map/all_to_all | solution.py:14
  50.1 1.9 %collective-permute-start.1 = (bf16[8,768]{1,0:T(8,128)(2,1)S(1)}, bf16[8,768]{1,0:T(8,128)(2,1)S(1)}, u32[]{:S(2)}, u32[]{:S(2)}) collective-permute-start(bf16[8,768]{1,0:T(8,128)(2,1)S(1)} %get-tuple-element.4), channel_id=1, source_target_pairs={{0,4},{4,0},{1,5},{5,1},{2,6},{6,2},{3,7},{7,3},{8,12},{12,8},{9,1... | collective-permute-start | bytes 36872 | tf_op jit(solution)/shard_map/ppermute | solution.py:71
  54.7 0.6 broadcast_in_dim.102
  55.4 4.3 %all-to-all-start.1 = ((bf16[4,2,8,768]{3,2,1,0:T(8,128)(2,1)}), bf16[4,2,8,768]{3,2,1,0:T(8,128)(2,1)S(1)}, u32[]{:S(2)}, u32[]{:S(2)}) async-start(bf16[4,2,8,768]{3,2,1,0:T(8,128)(2,1)} %broadcast_in_dim.102), calls=%async_computation.1 | async-start | bytes 196608 | tf_op jit(solution)/shard_map/all_to_all | solution.py:14
  59.7 7.0 %all-to-all-done.1 = bf16[4,2,8,768]{3,2,1,0:T(8,128)(2,1)S(1)} async-done(((bf16[4,2,8,768]{3,2,1,0:T(8,128)(2,1)}), bf16[4,2,8,768]{3,2,1,0:T(8,128)(2,1)S(1)}, u32[]{:S(2)}, u32[]{:S(2)}) %all-to-all-start.1) | async-done | bytes 98336 | tf_op jit(solution)/shard_map/all_to_all | solution.py:14
  66.8 1.1 fusion.20
  67.9 5.9 %all-gather.2.cloned.1.call-done = bf16[3,1024,768]{2,1,0:T(8,128)(2,1)} async-done(((bf16[3,256,768]{2,1,0:T(8,128)(2,1)}), bf16[3,1024,768]{2,1,0:T(8,128)(2,1)}) %all-gather.2.cloned.1.call-update) | async-done | bytes 4718608 | tf_op jit(solution)/shard_map/all_gather | solution.py:58
  73.7 4.2 %fusion.3 = bf16[3,256,768]{2,1,0:T(8,128)(2,1)S(1)} fusion(bf16[3,1024,768]{2,1,0:T(8,128)(2,1)} %all-gather.2.cloned.1.call-done, bf16[3,256,1024]{2,1,0:T(8,128)(2,1)} %param.11, pred[3,1024]{1,0:T(4,128)(4,1)S(1)} %iota_compare_fusion), kind=kOutput, calls=%fused_computation.5 | convolution fusion | flops 1209335808 | bytes 7474176 | tf_op jit(solution)/shard_map/sfg,sgn->sfn/dot_general | solution.py:61
  78.0 0.5 fusion.13
  78.5 0.4 fusion.9
  79.1 0.7 pad_maximum_fusion
  79.8 3.4 %all-to-all-start.2 = ((bf16[8,2,8,768]{3,2,1,0:T(8,128)(2,1)}), bf16[8,2,8,768]{3,2,1,0:T(8,128)(2,1)S(1)}, u32[]{:S(2)}, u32[]{:S(2)}) async-start(bf16[8,2,8,768]{3,2,1,0:T(8,128)(2,1)} %bitcast.20), calls=%async_computation.2 | async-start | bytes 393216 | tf_op jit(solution)/shard_map/all_to_all | solution.py:105
  83.2 6.2 %all-to-all-done.2 = bf16[8,2,8,768]{3,2,1,0:T(8,128)(2,1)S(1)} async-done(((bf16[8,2,8,768]{3,2,1,0:T(8,128)(2,1)}), bf16[8,2,8,768]{3,2,1,0:T(8,128)(2,1)S(1)}, u32[]{:S(2)}, u32[]{:S(2)}) %all-to-all-start.2) | async-done | bytes 196640 | tf_op jit(solution)/shard_map/all_to_all | solution.py:105
  89.6 1.3 add_convert_fusion
  90.8 13.4 %all-to-all-start.3 = ((bf16[64,8,768]{2,1,0:T(8,128)(2,1)}), bf16[64,8,768]{2,1,0:T(8,128)(2,1)S(1)}, u32[]{:S(2)}, u32[]{:S(2)}) async-start(bf16[64,8,768]{2,1,0:T(8,128)(2,1)} %add_convert_fusion), calls=%async_computation.3 | async-start | bytes 1572864 | tf_op jit(solution)/shard_map/all_to_all | solution.py:120
  104.2 0.2 rev.3
  104.6 23.9 %all-to-all-done.3 = bf16[64,8,768]{2,1,0:T(8,128)(2,1)S(1)} async-done(((bf16[64,8,768]{2,1,0:T(8,128)(2,1)}), bf16[64,8,768]{2,1,0:T(8,128)(2,1)S(1)}, u32[]{:S(2)}, u32[]{:S(2)}) %all-to-all-start.3) | async-done | bytes 786464 | tf_op jit(solution)/shard_map/all_to_all | solution.py:120
  128.6 0.7 fusion.24
  (47 shorter events, 0.7 us)
Async XLA Ops:
  7.2 59.6 %copy-start = (bf16[3,192,768]{2,1,0:T(8,128)(2,1)S(1)}, bf16[3,192,768]{2,1,0:T(8,128)(2,1)}, u32[]{:S(2)}) copy-start(bf16[3,192,768]{2,1,0:T(8,128)(2,1)} %param.13) | copy-start | bytes 2654212
  7.2 19.0 %copy-start.10 = (s32[3,1]{0,1:T(1,128)S(1)}, s32[3,1]{0,1:T(1,128)}, u32[]{:S(2)}) copy-start(s32[3,1]{0,1:T(1,128)} %param.10) | copy-start | bytes 40
  7.2 21.5 %copy-start.9 = (s32[3]{0:T(128)S(1)}, s32[3]{0:T(128)}, u32[]{:S(2)}) copy-start(s32[3]{0:T(128)} %param.9) | copy-start | bytes 40
  7.2 66.5 %all-gather.2.cloned.1.call-start = ((), (), s32[]{:S(2)}) async-start(), calls=%async_computation.4 | async-start | bytes 5898240 | tf_op jit(solution)/shard_map/all_gather | solution.py:58
  9.6 40.6 %all-to-all-start = ((bf16[64,8,768]{2,1,0:T(8,128)(2,1)}), bf16[64,8,768]{2,1,0:T(8,128)(2,1)S(1)}, u32[]{:S(2)}, u32[]{:S(2)}) async-start(bf16[64,8,768]{2,1,0:T(8,128)(2,1)} %broadcast_in_dim.101), calls=%async_computation | async-start | bytes 1572864 | tf_op jit(solution)/shard_map/all_to_all | solution.py:14
  26.8 3.1 %collective-permute-start = (s32[1]{0:T(128)}, s32[1]{0:T(128)}, u32[]{:S(2)}, u32[]{:S(2)}) collective-permute-start(s32[1]{0:T(128)} %bitcast.3), channel_id=1, source_target_pairs={{0,4},{4,0},{1,5},{5,1},{2,6},{6,2},{3,7},{7,3},{8,12},{12,8},{9,1... | collective-permute-start | bytes 20 | tf_op jit(solution)/shard_map/ppermute | solution.py:69
  50.1 4.6 %collective-permute-start.1 = (bf16[8,768]{1,0:T(8,128)(2,1)S(1)}, bf16[8,768]{1,0:T(8,128)(2,1)S(1)}, u32[]{:S(2)}, u32[]{:S(2)}) collective-permute-start(bf16[8,768]{1,0:T(8,128)(2,1)S(1)} %get-tuple-element.4), channel_id=1, source_target_pairs={{0,4},{4,0},{1,5},{5,1},{2,6},{6,2},{3,7},{7,3},{8,12},{12,8},{9,1... | collective-permute-start | bytes 36872 | tf_op jit(solution)/shard_map/ppermute | solution.py:71
  55.4 11.4 %all-to-all-start.1 = ((bf16[4,2,8,768]{3,2,1,0:T(8,128)(2,1)}), bf16[4,2,8,768]{3,2,1,0:T(8,128)(2,1)S(1)}, u32[]{:S(2)}, u32[]{:S(2)}) async-start(bf16[4,2,8,768]{3,2,1,0:T(8,128)(2,1)} %broadcast_in_dim.102), calls=%async_computation.1 | async-start | bytes 196608 | tf_op jit(solution)/shard_map/all_to_all | solution.py:14
  67.9 10.6 %copy-start.1 = (bf16[3,256,768]{2,1,0:T(8,128)(2,1)S(1)}, bf16[3,256,768]{2,1,0:T(8,128)(2,1)}, u32[]{:S(2)}) copy-start(bf16[3,256,768]{2,1,0:T(8,128)(2,1)} %param.12) | copy-start | bytes 3538948
  73.7 4.8 %copy-start.3 = (f32[3,32,768]{2,1,0:T(8,128)S(1)}, f32[3,32,768]{2,1,0:T(8,128)}, u32[]{:S(2)}) copy-start(f32[3,32,768]{2,1,0:T(8,128)} %fusion.20) | copy-start | bytes 884740
  78.0 1.0 copy-start.2
  78.5 1.3 copy-start.5
  79.8 9.7 %all-to-all-start.2 = ((bf16[8,2,8,768]{3,2,1,0:T(8,128)(2,1)}), bf16[8,2,8,768]{3,2,1,0:T(8,128)(2,1)S(1)}, u32[]{:S(2)}, u32[]{:S(2)}) async-start(bf16[8,2,8,768]{3,2,1,0:T(8,128)(2,1)} %bitcast.20), calls=%async_computation.2 | async-start | bytes 393216 | tf_op jit(solution)/shard_map/all_to_all | solution.py:105
  83.2 21.0 %copy-start.4 = (bf16[1,8,768]{2,1,0:T(8,128)(2,1)S(1)}, bf16[1,8,768]{2,1,0:T(8,128)(2,1)}, u32[]{:S(2)}) copy-start(bf16[1,8,768]{2,1,0:T(8,128)(2,1)} %param.14) | copy-start | bytes 36868
  89.5 15.0 %copy-start.7 = (f32[1,768]{1,0:T(1,128)S(1)}, f32[1,768]{1,0:T(1,128)}, u32[]{:S(2)}) copy-start(f32[1,768]{1,0:T(1,128)} %param.17) | copy-start | bytes 9220
  89.5 15.0 %copy-start.8 = (f32[1,768]{1,0:T(1,128)S(1)}, f32[1,768]{1,0:T(1,128)}, u32[]{:S(2)}) copy-start(f32[1,768]{1,0:T(1,128)} %param.16) | copy-start | bytes 9220
  89.6 39.0 %copy-start.6 = (f32[1,8,768]{2,1,0:T(8,128)S(1)}, f32[1,8,768]{2,1,0:T(8,128)}, u32[]{:S(2)}) copy-start(f32[1,8,768]{2,1,0:T(8,128)} %param.15) | copy-start | bytes 73732
  90.8 37.6 %all-to-all-start.3 = ((bf16[64,8,768]{2,1,0:T(8,128)(2,1)}), bf16[64,8,768]{2,1,0:T(8,128)(2,1)S(1)}, u32[]{:S(2)}, u32[]{:S(2)}) async-start(bf16[64,8,768]{2,1,0:T(8,128)(2,1)} %add_convert_fusion), calls=%async_computation.3 | async-start | bytes 1572864 | tf_op jit(solution)/shard_map/all_to_all | solution.py:120
Sparse Core Ops, SparseCore 0:
  10.1 63.5 all-gather.1
where the time goes:
time: 137 us; the launch traced here: 136 us
  waiting for transfers between devices  62.5 us (46%)
  starting transfers between devices  41.5 us (30%)
  between operations  19.6 us (14%)
  matrix products  6.18 us (5%)
  local copies, waits for them, and re-layouts  3.31 us (2%)
  other arithmetic  3.12 us (2%)
    all_to_all x2, waiting for transfers between devices, copy_for_each(): lax.all_to_all(jnp.broadcast_to(x[None], (length, *x.shape)), axis, 0, 0,...  24.7 us
    all_to_all x1, waiting for transfers between devices, body(): lax.all_to_all(dense.astype(jnp.bfloat16), PLANE, split_axis=0, concat_ax...  23.9 us
    all_to_all x2, starting transfers between devices, copy_for_each(): lax.all_to_all(jnp.broadcast_to(x[None], (length, *x.shape)), axis, 0, 0,...  20.9 us
    all_to_all x1, starting transfers between devices, body(): lax.all_to_all(dense.astype(jnp.bfloat16), PLANE, split_axis=0, concat_ax...  13.4 us
    all_to_all x1, waiting for transfers between devices, body(): lax.all_to_all(send.reshape(2 * nharm, 2, rows_q, width).astype(jnp.bfloa...  6.23 us
    all_gather x1, waiting for transfers between devices, body(): piece = lax.all_gather(coupling, 'harm', axis=1, tiled=True)  5.86 us
    dot_general x1, matrix products, body(): jnp.einsum('sfg,sgn->sfn', front_live, piece, preferred_element_type=jnp....  4.24 us
    all_to_all x1, starting transfers between devices, body(): lax.all_to_all(send.reshape(2 * nharm, 2, rows_q, width).astype(jnp.bfloa...  3.42 us
  transfers between devices with their start and end apart: 7, of which 6 were waited for; matrix products, arithmetic and copies ran while one was open for 3% of the time, Pallas kernels for 0%

commit v1 on v0

--- a/solution.py
+++ b/solution.py
@@ -55,7 +55,9 @@
     own_rows = harm_idx * front_q + jnp.arange(front_q, dtype=jnp.int32)
     live_rows = own_rows[None, :] < lengths[:, None]
     masked = jnp.where(live_rows[:, :, None], coupling, jnp.zeros_like(coupling))
-    piece = lax.all_gather(coupling, "harm", axis=1, tiled=True)
+    piece = jnp.concatenate(
+        lax.all_to_all(jnp.stack([coupling] * lax.axis_size("harm")), "harm", 0, 0), axis=1
+    )
     live_cols = jnp.arange(nharm * front_q, dtype=jnp.int32)[None, :] < lengths[:, None]
     front_live = jnp.where(live_cols[:, None, :], front_inverse, jnp.zeros_like(front_inverse))
     modes = jnp.einsum(

time: 137 us -> 168 us (1.23)
  waiting for transfers between devices: 62.5 us -> 102 us
  between operations: 19.6 us -> 6.46 us
  blocking collectives: 0 us -> 9.89 us
  starting transfers between devices: 41.5 us -> 35.5 us
  local copies, waits for them, and re-layouts: 3.31 us -> 8.24 us
  matrix products: 6.18 us -> 2.62 us
    all_to_all x0 -> x1, waiting for transfers between devices: none -> 53.4 us  [body(): lax.all_to_all(jnp.stack([coupling] * lax.axis_size('harm')), 'harm', 0, 0)]
    all_to_all x0 -> x1, blocking collectives: none -> 9.89 us  [copy_for_each(): lax.all_to_all(jnp.broadcast_to(x[None], (length, *x.shape)), axis, 0, 0,...]
    all_to_all x2 -> x1, waiting for transfers between devices: 24.7 us -> 17.5 us  [copy_for_each(): lax.all_to_all(jnp.broadcast_to(x[None], (length, *x.shape)), axis, 0, 0,...]
    all_to_all x1, starting transfers between devices: 13.4 us -> 6.56 us  [body(): lax.all_to_all(dense.astype(jnp.bfloat16), PLANE, split_axis=0, concat_ax...]
    all_gather x1 -> x0, waiting for transfers between devices: 5.86 us -> none  [body(): piece = lax.all_gather(coupling, 'harm', axis=1, tiled=True)]
    all_to_all x0 -> x1, starting transfers between devices: none -> 5.1 us  [body(): lax.all_to_all(jnp.stack([coupling] * lax.axis_size('harm')), 'harm', 0, 0)]
    all_to_all x2 -> x1, starting transfers between devices: 20.9 us -> 16.6 us  [copy_for_each(): lax.all_to_all(jnp.broadcast_to(x[None], (length, *x.shape)), axis, 0, 0,...]
    dot_general x1, matrix products: 4.24 us -> 1.39 us  [body(): jnp.einsum('sfg,sgn->sfn', front_live, piece, preferred_element_type=jnp....]
  transfers between devices with their start and end apart: 7 -> 6, of which waited for: 6 -> 5; matrix products, arithmetic and copies ran while one was open for 3% -> 1% of each run, Pallas kernels for 0% -> 0%
where the time goes in v1:
time: 168 us
  waiting for transfers between devices  102 us (61%)
  starting transfers between devices  35.5 us (21%)
  blocking collectives  9.89 us (6%)
  local copies, waits for them, and re-layouts  8.24 us (5%)
  between operations  6.46 us (4%)
  other arithmetic  3.13 us (2%)
  matrix products  2.62 us (2%)
    all_to_all x1, waiting for transfers between devices, body(): lax.all_to_all(jnp.stack([coupling] * lax.axis_size('harm')), 'harm', 0, 0)  53.4 us
    all_to_all x1, waiting for transfers between devices, body(): lax.all_to_all(dense.astype(jnp.bfloat16), PLANE, split_axis=0, concat_ax...  23.9 us
    all_to_all x1, waiting for transfers between devices, copy_for_each(): lax.all_to_all(jnp.broadcast_to(x[None], (length, *x.shape)), axis, 0, 0,...  17.5 us
    all_to_all x1, starting transfers between devices, copy_for_each(): lax.all_to_all(jnp.broadcast_to(x[None], (length, *x.shape)), axis, 0, 0,...  16.6 us
    all_to_all x1, blocking collectives, copy_for_each(): lax.all_to_all(jnp.broadcast_to(x[None], (length, *x.shape)), axis, 0, 0,...  9.89 us
    all_to_all x1, starting transfers between devices, body(): lax.all_to_all(dense.astype(jnp.bfloat16), PLANE, split_axis=0, concat_ax...  6.56 us
    all_to_all x1, waiting for transfers between devices, body(): lax.all_to_all(send.reshape(2 * nharm, 2, rows_q, width).astype(jnp.bfloa...  6.15 us
    all_to_all x1, starting transfers between devices, body(): lax.all_to_all(jnp.stack([coupling] * lax.axis_size('harm')), 'harm', 0, 0)  5.1 us
  transfers between devices with their start and end apart: 6, of which 5 were waited for; matrix products, arithmetic and copies ran while one was open for 1% of the time, Pallas kernels for 0%

profile of v1, /device:TPU:8, one launch (start us, length us, event | category | flops | bytes accessed | tf_op | source)
XLA Modules:
  0.0 167.8 jit_solution(13931360056682022554)
XLA Ops:
  0.7 1.8 %broadcast_in_dim.101 = bf16[64,8,768]{2,1,0:T(8,128)(2,1)} broadcast(bf16[8,768]{1,0:T(8,128)(2,1)} %bitcast.61), dimensions={1,2} | broadcast | bytes 798720 | tf_op jit(solution)/shard_map/broadcast_in_dim | solution.py:14
  2.4 16.6 %all-to-all-start = ((bf16[64,8,768]{2,1,0:T(8,128)(2,1)}), bf16[64,8,768]{2,1,0:T(8,128)(2,1)S(1)}, u32[]{:S(2)}, u32[]{:S(2)}) async-start(bf16[64,8,768]{2,1,0:T(8,128)(2,1)} %broadcast_in_dim.101), calls=%async_computation | async-start | bytes 1572864 | tf_op jit(solution)/shard_map/all_to_all | solution.py:14
  19.0 0.6 slice.46
  19.6 1.9 %collective-permute-start = (s32[1]{0:T(128)}, s32[1]{0:T(128)}, u32[]{:S(2)}, u32[]{:S(2)}) collective-permute-start(s32[1]{0:T(128)} %bitcast.3), channel_id=1, source_target_pairs={{0,4},{4,0},{1,5},{5,1},{2,6},{6,2},{3,7},{7,3},{8,12},{12,8},{9,1... | collective-permute-start | bytes 20 | tf_op jit(solution)/shard_map/ppermute | solution.py:71
  21.6 1.2 collective-permute-done
  25.5 17.5 %all-to-all-done = bf16[64,8,768]{2,1,0:T(8,128)(2,1)S(1)} async-done(((bf16[64,8,768]{2,1,0:T(8,128)(2,1)}), bf16[64,8,768]{2,1,0:T(8,128)(2,1)S(1)}, u32[]{:S(2)}, u32[]{:S(2)}) %all-to-all-start) | async-done | bytes 786464 | tf_op jit(solution)/shard_map/all_to_all | solution.py:14
  43.0 1.9 %collective-permute-start.1 = (bf16[8,768]{1,0:T(8,128)(2,1)S(1)}, bf16[8,768]{1,0:T(8,128)(2,1)S(1)}, u32[]{:S(2)}, u32[]{:S(2)}) collective-permute-start(bf16[8,768]{1,0:T(8,128)(2,1)S(1)} %get-tuple-element.4), channel_id=1, source_target_pairs={{0,4},{4,0},{1,5},{5,1},{2,6},{6,2},{3,7},{7,3},{8,12},{12,8},{9,1... | collective-permute-start | bytes 36872 | tf_op jit(solution)/shard_map/ppermute | solution.py:73
  47.6 9.9 %all_to_all.25 = bf16[4,2,8,768]{3,2,1,0:T(8,128)(2,1)S(1)} all-to-all(bf16[4,2,8,768]{3,2,1,0:T(8,128)(2,1)S(1)} %broadcast_in_dim.102), channel_id=1, replica_groups=mesh['sub_0'=8,'sub_1'=8,'sub_2'=2,'harm'=4] {'harm'}, dimensions={0} | all-to-all | bytes 196608 | tf_op jit(solution)/shard_map/all_to_all | solution.py:14
  57.5 2.6 %stack.44 = bf16[4,3,256,768]{3,2,1,0:T(8,128)(2,1)} broadcast(bf16[3,256,768]{2,1,0:T(8,128)(2,1)S(1)} %copy-done.2), dimensions={1,2,3} | broadcast | bytes 5898240 | tf_op jit(solution)/shard_map/stack | solution.py:59
  60.1 5.1 %all-to-all-start.2 = ((bf16[4,3,256,768]{3,2,1,0:T(8,128)(2,1)}), bf16[4,3,256,768]{3,2,1,0:T(8,128)(2,1)}, u32[]{:S(2)}, u32[]{:S(2)}) async-start(bf16[4,3,256,768]{3,2,1,0:T(8,128)(2,1)} %stack.44), calls=%async_computation.2 | async-start | bytes 9437184 | tf_op jit(solution)/shard_map/all_to_all | solution.py:59
  65.4 0.3 fusion.20
  65.8 53.4 %all-to-all-done.2 = bf16[4,3,256,768]{3,2,1,0:T(8,128)(2,1)} async-done(((bf16[4,3,256,768]{3,2,1,0:T(8,128)(2,1)}), bf16[4,3,256,768]{3,2,1,0:T(8,128)(2,1)}, u32[]{:S(2)}, u32[]{:S(2)}) %all-to-all-start.2) | async-done | bytes 4718624 | tf_op jit(solution)/shard_map/all_to_all | solution.py:59
  119.2 2.8 %copy.21 = bf16[3,4,256,768]{3,2,1,0:T(8,128)(2,1)S(1)} copy(bf16[3,4,256,768]{3,2,0,1:T(8,128)(2,1)} %bitcast.10) | data formatting | bytes 9437184 | tf_op jit(solution)/shard_map/reshape | solution.py:58
  122.0 1.4 fusion.3
  123.4 0.5 fusion.13
  124.0 0.4 fusion.9
  124.5 0.7 pad_maximum_fusion
  125.2 3.4 %all-to-all-start.3 = ((bf16[8,2,8,768]{3,2,1,0:T(8,128)(2,1)}), bf16[8,2,8,768]{3,2,1,0:T(8,128)(2,1)S(1)}, u32[]{:S(2)}, u32[]{:S(2)}) async-start(bf16[8,2,8,768]{3,2,1,0:T(8,128)(2,1)} %bitcast.22), calls=%async_computation.3 | async-start | bytes 393216 | tf_op jit(solution)/shard_map/all_to_all | solution.py:107
  128.7 6.1 %all-to-all-done.3 = bf16[8,2,8,768]{3,2,1,0:T(8,128)(2,1)S(1)} async-done(((bf16[8,2,8,768]{3,2,1,0:T(8,128)(2,1)}), bf16[8,2,8,768]{3,2,1,0:T(8,128)(2,1)S(1)}, u32[]{:S(2)}, u32[]{:S(2)}) %all-to-all-start.3) | async-done | bytes 196640 | tf_op jit(solution)/shard_map/all_to_all | solution.py:107
  134.9 1.3 add_convert_fusion
  136.2 6.6 %all-to-all-start.4 = ((bf16[64,8,768]{2,1,0:T(8,128)(2,1)}), bf16[64,8,768]{2,1,0:T(8,128)(2,1)S(1)}, u32[]{:S(2)}, u32[]{:S(2)}) async-start(bf16[64,8,768]{2,1,0:T(8,128)(2,1)} %add_convert_fusion), calls=%async_computation.4 | async-start | bytes 1572864 | tf_op jit(solution)/shard_map/all_to_all | solution.py:122
  142.8 0.2 rev.3
  143.1 23.9 %all-to-all-done.4 = bf16[64,8,768]{2,1,0:T(8,128)(2,1)S(1)} async-done(((bf16[64,8,768]{2,1,0:T(8,128)(2,1)}), bf16[64,8,768]{2,1,0:T(8,128)(2,1)S(1)}, u32[]{:S(2)}, u32[]{:S(2)}) %all-to-all-start.4) | async-done | bytes 786464 | tf_op jit(solution)/shard_map/all_to_all | solution.py:122
  167.2 0.7 fusion.24
  (49 shorter events, 0.8 us)
Async XLA Ops:
  0.6 64.8 %copy-start = (bf16[3,192,768]{2,1,0:T(8,128)(2,1)S(1)}, bf16[3,192,768]{2,1,0:T(8,128)(2,1)}, u32[]{:S(2)}) copy-start(bf16[3,192,768]{2,1,0:T(8,128)(2,1)} %param.13) | copy-start | bytes 2654212
  0.6 18.4 %copy-start.11 = (s32[3,1]{0,1:T(1,128)S(1)}, s32[3,1]{0,1:T(1,128)}, u32[]{:S(2)}) copy-start(s32[3,1]{0,1:T(1,128)} %param.10) | copy-start | bytes 40
  0.7 56.8 %copy-start.2 = (bf16[3,256,768]{2,1,0:T(8,128)(2,1)S(1)}, bf16[3,256,768]{2,1,0:T(8,128)(2,1)}, u32[]{:S(2)}) copy-start(bf16[3,256,768]{2,1,0:T(8,128)(2,1)} %param.12) | copy-start | bytes 3538948
  2.4 40.6 %all-to-all-start = ((bf16[64,8,768]{2,1,0:T(8,128)(2,1)}), bf16[64,8,768]{2,1,0:T(8,128)(2,1)S(1)}, u32[]{:S(2)}, u32[]{:S(2)}) async-start(bf16[64,8,768]{2,1,0:T(8,128)(2,1)} %broadcast_in_dim.101), calls=%async_computation | async-start | bytes 1572864 | tf_op jit(solution)/shard_map/all_to_all | solution.py:14
  19.6 3.1 %collective-permute-start = (s32[1]{0:T(128)}, s32[1]{0:T(128)}, u32[]{:S(2)}, u32[]{:S(2)}) collective-permute-start(s32[1]{0:T(128)} %bitcast.3), channel_id=1, source_target_pairs={{0,4},{4,0},{1,5},{5,1},{2,6},{6,2},{3,7},{7,3},{8,12},{12,8},{9,1... | collective-permute-start | bytes 20 | tf_op jit(solution)/shard_map/ppermute | solution.py:71
  43.0 4.5 %collective-permute-start.1 = (bf16[8,768]{1,0:T(8,128)(2,1)S(1)}, bf16[8,768]{1,0:T(8,128)(2,1)S(1)}, u32[]{:S(2)}, u32[]{:S(2)}) collective-permute-start(bf16[8,768]{1,0:T(8,128)(2,1)S(1)} %get-tuple-element.4), channel_id=1, source_target_pairs={{0,4},{4,0},{1,5},{5,1},{2,6},{6,2},{3,7},{7,3},{8,12},{12,8},{9,1... | collective-permute-start | bytes 36872 | tf_op jit(solution)/shard_map/ppermute | solution.py:73
  60.1 5.1 %copy-start.9 = (s32[3]{0:T(128)S(1)}, s32[3]{0:T(128)}, u32[]{:S(2)}) copy-start(s32[3]{0:T(128)} %param.9) | copy-start | bytes 40
  60.1 59.1 %all-to-all-start.2 = ((bf16[4,3,256,768]{3,2,1,0:T(8,128)(2,1)}), bf16[4,3,256,768]{3,2,1,0:T(8,128)(2,1)}, u32[]{:S(2)}, u32[]{:S(2)}) async-start(bf16[4,3,256,768]{3,2,1,0:T(8,128)(2,1)} %stack.44), calls=%async_computation.2 | async-start | bytes 9437184 | tf_op jit(solution)/shard_map/all_to_all | solution.py:59
  119.2 2.8 %copy-start.10 = (bf16[3,256,1024]{2,1,0:T(8,128)(2,1)S(1)}, bf16[3,256,1024]{2,1,0:T(8,128)(2,1)}, u32[]{:S(2)}) copy-start(bf16[3,256,1024]{2,1,0:T(8,128)(2,1)} %param.11) | copy-start | bytes 4718596
  122.0 1.9 %copy-start.3 = (bf16[3,256,768]{2,1,0:T(8,128)(2,1)S(1)}, bf16[3,256,768]{2,1,0:T(8,128)(2,1)}, u32[]{:S(2)}) copy-start(bf16[3,256,768]{2,1,0:T(8,128)(2,1)} %param.12) | copy-start | bytes 3538948
  123.4 1.0 copy-start.1
  123.9 1.3 copy-start.5
  125.2 9.6 %all-to-all-start.3 = ((bf16[8,2,8,768]{3,2,1,0:T(8,128)(2,1)}), bf16[8,2,8,768]{3,2,1,0:T(8,128)(2,1)S(1)}, u32[]{:S(2)}, u32[]{:S(2)}) async-start(bf16[8,2,8,768]{3,2,1,0:T(8,128)(2,1)} %bitcast.22), calls=%async_computation.3 | async-start | bytes 393216 | tf_op jit(solution)/shard_map/all_to_all | solution.py:107
  128.7 14.1 %copy-start.4 = (bf16[1,8,768]{2,1,0:T(8,128)(2,1)S(1)}, bf16[1,8,768]{2,1,0:T(8,128)(2,1)}, u32[]{:S(2)}) copy-start(bf16[1,8,768]{2,1,0:T(8,128)(2,1)} %param.14) | copy-start | bytes 36868
  134.8 8.2 %copy-start.7 = (f32[1,768]{1,0:T(1,128)S(1)}, f32[1,768]{1,0:T(1,128)}, u32[]{:S(2)}) copy-start(f32[1,768]{1,0:T(1,128)} %param.17) | copy-start | bytes 9220
  134.9 8.2 %copy-start.8 = (f32[1,768]{1,0:T(1,128)S(1)}, f32[1,768]{1,0:T(1,128)}, u32[]{:S(2)}) copy-start(f32[1,768]{1,0:T(1,128)} %param.16) | copy-start | bytes 9220
  134.9 32.2 %copy-start.6 = (f32[1,8,768]{2,1,0:T(8,128)S(1)}, f32[1,8,768]{2,1,0:T(8,128)}, u32[]{:S(2)}) copy-start(f32[1,8,768]{2,1,0:T(8,128)} %param.15) | copy-start | bytes 73732
  136.2 30.8 %all-to-all-start.4 = ((bf16[64,8,768]{2,1,0:T(8,128)(2,1)}), bf16[64,8,768]{2,1,0:T(8,128)(2,1)S(1)}, u32[]{:S(2)}, u32[]{:S(2)}) async-start(bf16[64,8,768]{2,1,0:T(8,128)(2,1)} %add_convert_fusion), calls=%async_computation.4 | async-start | bytes 1572864 | tf_op jit(solution)/shard_map/all_to_all | solution.py:122
